TPU v7x, 128 devices: a whole 4x4x4 slice. The times are simulated.
128 devices in a mesh: seq: 16 (over y, x), grp: 8 (over z, core).
Axes of the slice: x: 4, y: 4, z: 4, core: 2. Of those that a mesh axis runs over, the one named last changes fastest.
Arguments:
- patches: bfloat16 [16384, 1664], P(('grp', 'seq')), may hold values from -6 to 6
- vis_gain: float32 [1664], replicated, may hold values from 0.25 to 1.75
- vis_qkv: bfloat16 [3, 1664, 1664], P(None, None, 'seq')
- vis_out: bfloat16 [1664, 1664], P('seq'), may hold values from -0.15625 to 0.15625
- merge_gain: float32 [1664], replicated, may hold values from 0.25 to 1.75
- merge_w: bfloat16 [6656, 1664], P('seq'), may hold values from -0.078125 to 0.078125
- image_blocks: int32 [8, 4], P('grp'), may hold values from 1 to 256, 512 in all within a row
- dest_group: int32 [4096, 1], P(('grp', 'seq')), may hold values from 0 to 7; in each aligned block of 32 rows (0 to 31, 32 to 63, ...) at most 8 rows name the same one
- slot_rows: int32 [8, 16, 128], P('grp', 'seq'), may hold values from 0 to 127, each once within a row
- prompt_len: int32 [8], P('grp'), may hold values from 512 to 2048
- text_emb: bfloat16 [16384, 1664], P(('grp', 'seq')), may hold values from -6 to 6
- txt_gain: float32 [1664], replicated, may hold values from 0.25 to 1.75
- txt_qkv: bfloat16 [3, 1664, 1664], P(None, None, 'seq')
- txt_out: bfloat16 [1664, 1664], P('seq'), may hold values from -0.15625 to 0.15625
Outputs:
- text_out: float32 [16384, 1664], P(('grp', 'seq'))
Inputs may be any that keep to these rules, and one draw needn't show every extreme that they name: image_blocks[g] sum to 512; one image of every group has the most. `dest_group`: of the 32 merged tokens of one device (aligned blocks of rows), at most 8 name one group. slot_rows[q, s] is a permutation of 0 to 127.
All inputs are finite; a program needn't handle non-finite values.
Results may differ from a plain program's by a relative error of at most 0.012.
Values may be sent and summed in bfloat16 or wider, within the bound.
No kernel may reach another device: no remote copies, remote signals or barrier semaphores. Data moves between devices by JAX's collectives and lax.ppermute only.
A program may use at most 64 MiB of HBM per device.

v0:
```python
import jax
import jax.numpy as jnp
from jax import lax
from jax.sharding import PartitionSpec as P

HEAD_DIM = 104


def layer_norm(row_block, scale_gain):
    values_f = row_block.astype(jnp.float32)
    row_mean = jnp.mean(values_f, axis=-1, keepdims=True)
    centred = values_f - row_mean
    variance = jnp.mean(centred * centred, axis=-1, keepdims=True)
    return centred * lax.rsqrt(variance + 1e-06) * scale_gain


def rms_norm(row_block, scale_gain):
    values_f = row_block.astype(jnp.float32)
    return (
        values_f
        * lax.rsqrt(jnp.mean(values_f * values_f, axis=-1, keepdims=True) + 1e-06)
        * scale_gain
    )


def projector(weights, shard_piece):
    count, width, head_width = weights.shape
    packed = weights.transpose(1, 0, 2).reshape(width, count * head_width)
    joined = jnp.dot(shard_piece, packed, preferred_element_type=jnp.float32).astype(jnp.bfloat16)
    return joined.reshape(shard_piece.shape[0], count, head_width).transpose(1, 0, 2)


def attend_local(queries, key_rows, value_rows, allowed_fn):
    length = queries.shape[0]
    head_width = queries.shape[1]
    head_count = head_width // HEAD_DIM
    block_rows = min(512, length)
    block_count = length // block_rows
    query_blocks = queries.reshape(block_count, block_rows, head_count, HEAD_DIM)
    key_heads = key_rows.reshape(length, head_count, HEAD_DIM)
    value_heads = value_rows.reshape(length, head_count, HEAD_DIM)

    def one_block(block_item):
        query_part, first_row = block_item
        scores = jnp.einsum(
            "qhe,khe->hqk", query_part, key_heads, preferred_element_type=jnp.float32
        ) * HEAD_DIM ** (-0.5)
        allowed = allowed_fn(first_row + jnp.arange(block_rows, dtype=jnp.int32))
        scores = jnp.where(allowed[None], scores, -1e30)
        row_max = jnp.max(scores, axis=-1, keepdims=True)
        expo = jnp.exp(scores - row_max)
        probabilities = (expo / jnp.sum(expo, axis=-1, keepdims=True)).astype(jnp.bfloat16)
        return jnp.einsum(
            "hqk,khe->qhe", probabilities, value_heads, preferred_element_type=jnp.float32
        ).astype(jnp.bfloat16)

    starts = jnp.arange(block_count, dtype=jnp.int32) * block_rows
    joined = lax.map(one_block, (query_blocks, starts))
    return joined.reshape(length, head_width)


def heads_to_rows(heads, seq_count):
    length, width = heads.shape
    rows = length // seq_count
    blocks = heads.reshape(seq_count, rows, width)
    swapped = lax.all_to_all(blocks, "seq", split_axis=0, concat_axis=0, tiled=True)
    return swapped.transpose(1, 0, 2).reshape(rows, seq_count * width)


def attend_causal(queries, key_rows, value_rows, allowed_fn):
    length = queries.shape[0]
    head_width = queries.shape[1]
    head_count = head_width // HEAD_DIM
    block_rows = min(512, length)
    block_count = length // block_rows
    key_heads = key_rows.reshape(length, head_count, HEAD_DIM)
    value_heads = value_rows.reshape(length, head_count, HEAD_DIM)
    outputs = []
    for block in range(block_count):
        first_row = block * block_rows
        key_end = first_row + block_rows
        query_part = queries[first_row:key_end].reshape(block_rows, head_count, HEAD_DIM)
        scores = jnp.einsum(
            "qhe,khe->hqk", query_part, key_heads[:key_end], preferred_element_type=jnp.float32
        ) * HEAD_DIM ** (-0.5)
        allowed = allowed_fn(first_row + jnp.arange(block_rows, dtype=jnp.int32))[:, :key_end]
        scores = jnp.where(allowed[None], scores, -1e30)
        row_max = jnp.max(scores, axis=-1, keepdims=True)
        expo = jnp.exp(scores - row_max)
        probabilities = (expo / jnp.sum(expo, axis=-1, keepdims=True)).astype(jnp.bfloat16)
        outputs.append(
            jnp.einsum(
                "hqk,khe->qhe",
                probabilities,
                value_heads[:key_end],
                preferred_element_type=jnp.float32,
            ).astype(jnp.bfloat16)
        )
    return jnp.concatenate(outputs, axis=0).reshape(length, head_width)


def per_device(
    patches,
    vis_gain,
    vis_qkv,
    vis_out,
    merge_gain,
    merge_w,
    image_blocks,
    dest_group,
    slot_rows,
    prompt_len,
    text_emb,
    txt_gain,
    txt_qkv,
    txt_out,
):
    seq_count = lax.axis_size("seq")
    groups = lax.axis_size("grp")
    token_count = patches.shape[0]
    model_width = patches.shape[1]
    group_patches = token_count * seq_count
    vis_out_full = lax.all_gather(vis_out, "seq", axis=0, tiled=True)
    vis_normed = layer_norm(patches, vis_gain).astype(jnp.bfloat16)
    vis_proj = projector(vis_qkv, lax.all_gather(vis_normed, "seq", axis=0, tiled=True))
    bounds = jnp.cumsum(image_blocks[0])[:-1]

    def segment(indices):
        return jnp.sum(((indices // 4)[:, None] >= bounds[None, :]).astype(jnp.int32), axis=1)

    key_segments = segment(jnp.arange(group_patches, dtype=jnp.int32))

    def vis_allowed(row_indices):
        return segment(row_indices)[:, None] == key_segments[None, :]

    vis_heads = attend_local(vis_proj[0], vis_proj[1], vis_proj[2], vis_allowed)
    vis_heads, txt_out = lax.optimization_barrier((vis_heads, txt_out))
    txt_out_full = lax.all_gather(txt_out, "seq", axis=0, tiled=True)
    vis_attn = jnp.dot(
        heads_to_rows(vis_heads, seq_count), vis_out_full, preferred_element_type=jnp.float32
    )
    residual_sum = patches.astype(jnp.float32) + vis_attn
    merged_in = (
        layer_norm(residual_sum, merge_gain)
        .astype(jnp.bfloat16)
        .reshape(token_count // 4, 4 * model_width)
    )
    feature_slices = lax.all_to_all(merged_in, "seq", split_axis=1, concat_axis=0, tiled=True)
    merge_partial = jnp.dot(feature_slices, merge_w, preferred_element_type=jnp.float32)
    merge_parts = lax.all_to_all(
        merge_partial.astype(jnp.bfloat16).reshape(seq_count, -1, model_width),
        "seq",
        split_axis=0,
        concat_axis=0,
        tiled=True,
    )
    visual = jnp.sum(merge_parts.astype(jnp.float32), axis=0).astype(jnp.bfloat16)
    dest_rows = dest_group[:, 0]
    merged_rows = dest_rows.shape[0]
    capacity = max(2, 2 * merged_rows // groups)
    onehot = (dest_rows[:, None] == jnp.arange(groups, dtype=jnp.int32)[None, :]).astype(jnp.int32)
    slot_rank = jnp.sum((jnp.cumsum(onehot, axis=0) - 1) * onehot, axis=1)
    selector = (
        (dest_rows[None, None, :] == jnp.arange(groups, dtype=jnp.int32)[:, None, None])
        & (slot_rank[None, None, :] == jnp.arange(capacity, dtype=jnp.int32)[None, :, None])
    ).astype(jnp.bfloat16)
    outgoing = jnp.einsum(
        "gct,td->gcd", selector, visual, preferred_element_type=jnp.float32
    ).astype(jnp.bfloat16)
    arrived_flags = jnp.sum(selector.astype(jnp.float32), axis=2).astype(jnp.bfloat16)
    flag_row = jnp.pad(arrived_flags, ((0, 0), (0, model_width - capacity)))[:, None, :]
    payload = lax.all_to_all(
        jnp.concatenate([outgoing, flag_row], axis=1),
        "grp",
        split_axis=0,
        concat_axis=0,
        tiled=True,
    )
    incoming = payload[:, :capacity, :]
    arrived = payload[:, capacity, :capacity]
    prompt_rows = text_emb.shape[0]
    slot_targets = slot_rows[0, 0, : groups * capacity]
    placement_map = (
        slot_targets[None, :] == jnp.arange(prompt_rows, dtype=jnp.int32)[:, None]
    ).astype(jnp.bfloat16)
    placement_map = placement_map * arrived.reshape(1, groups * capacity)
    replaced = jnp.sum(placement_map.astype(jnp.float32), axis=1, keepdims=True)
    placed = jnp.dot(
        placement_map,
        incoming.reshape(groups * capacity, model_width),
        preferred_element_type=jnp.float32,
    )
    hidden = (text_emb.astype(jnp.float32) * (1.0 - replaced) + placed).astype(jnp.bfloat16)
    txt_normed = rms_norm(hidden, txt_gain).astype(jnp.bfloat16)
    txt_normed, txt_out_full = lax.optimization_barrier((txt_normed, txt_out_full))
    txt_proj = projector(txt_qkv, lax.all_gather(txt_normed, "seq", axis=0, tiled=True))
    length = prompt_len[0]
    key_positions = jnp.arange(prompt_rows * seq_count, dtype=jnp.int32)

    def txt_allowed(row_indices):
        return (key_positions[None, :] <= row_indices[:, None]) & (key_positions[None, :] < length)

    txt_heads = attend_causal(txt_proj[0], txt_proj[1], txt_proj[2], txt_allowed)
    txt_attn = jnp.dot(
        heads_to_rows(txt_heads, seq_count), txt_out_full, preferred_element_type=jnp.float32
    )
    return hidden.astype(jnp.float32) + txt_attn


def solution(mesh):
    in_specs = (
        P(("grp", "seq"), None),
        P(),
        P(None, None, "seq"),
        P("seq", None),
        P(),
        P("seq", None),
        P("grp", None),
        P(("grp", "seq"), None),
        P("grp", "seq", None),
        P("grp"),
        P(("grp", "seq"), None),
        P(),
        P(None, None, "seq"),
        P("seq", None),
    )
    out_specs = P(("grp", "seq"), None)
    return jax.shard_map(
        per_device, mesh=mesh, in_specs=in_specs, out_specs=out_specs, check_vma=False
    )
```

profile of v0, /device:TPU:0, one launch (start us, length us, event | category | flops | bytes accessed | tf_op | source)
XLA Modules:
  0.0 321.0 jit_solution(7446433832728544742)
XLA Ops:
  6.5 1.3 convert_reduce_fusion.1
  7.8 1.3 fusion.35
  9.1 2.1 fusion.37
  12.9 64.4 %all-gather.5.cloned.1.call-done = bf16[2048,1664]{1,0:T(8,128)(2,1)} async-done(((bf16[128,1664]{1,0:T(8,128)(2,1)}), bf16[2048,1664]{1,0:T(8,128)(2,1)}) %all-gather.5.cloned.1.call-update) | async-done | bytes 6815760 | tf_op jit(solution)/shard_map/all_gather | solution.py:125
  77.4 5.7 %convolution_convert_fusion.2 = bf16[2048,312]{0,1:T(8,128)(2,1)S(1)} fusion(bf16[2048,1664]{1,0:T(8,128)(2,1)} %all-gather.5.cloned.1.call-done, bf16[1664,312]{0,1:T(8,128)(2,1)} %bitcast.189), kind=kOutput, calls=%fused_computation.38 | convolution fusion | flops 2127151104 | bytes 9132032 | tf_op jit(solution)/shard_map/dot_general | solution.py:29
  83.6 16.5 %while.12 = (s32[]{:T(128)}, bf16[4,512,1,104]{1,3,2,0:T(8,128)(2,1)S(1)}, s32[4]{0:T(128)S(1)}, s32[3]{0:T(128)S(1)}, s32[2048]{0:T(1024)S(1)}, /*index=5*/bf16...) while((s32[]{:T(128)}, ...), condition=%wide.region_10.11_spmd, body=%wide.region_6.10_spmd.sunk | while | flops 445709312 | bytes 13674625 | solution.py:58
  90.8 1.1 fusion.77
  94.9 1.1 fusion.77
  101.3 5.3 %all-to-all-start = ((bf16[16,128,104]{1,2,0:T(8,128)(2,1)}), bf16[16,128,104]{1,2,0:T(8,128)(2,1)S(1)}, u32[]{:S(2)}, u32[]{:S(2)}) async-start(bf16[16,128,104]{1,2,0:T(8,128)(2,1)} %copy_bitcast_fusion), calls=%async_computation | async-start | bytes 851968 | tf_op jit(solution)/shard_map/all_to_all | solution.py:66
  106.6 31.9 %all-gather.7.cloned.1.call-done = bf16[1664,1664]{1,0:T(8,128)(2,1)} async-done(((bf16[104,1664]{1,0:T(8,128)(2,1)}), bf16[1664,1664]{1,0:T(8,128)(2,1)}) %all-gather.7.cloned.1.call-update) | async-done | bytes 5537808 | tf_op jit(solution)/shard_map/all_gather | solution.py:123
  138.5 3.7 %fusion.54 = (f32[128]{0:T(128)S(1)}, f32[128,1664]{1,0:T(8,128)S(1)}) fusion(bf16[128,1664]{0,1:T(8,128)(2,1)S(1)} %bitcast.177, bf16[1664,1664]{1,0:T(8,128)(2,1)} %all-gather.7.cloned.1.call-done, bf16[128,1664]{1,0:T(8,128)(2,1)S(1)} %copy-done.1), kind=kOutput, calls=%fused_computation.139 | convolution fusion | flops 709476224 | bytes 7242240 | tf_op jit(solution)/shard_map/dot_general | solution.py:139
  143.6 19.0 %all_to_all.39 = bf16[32,16,416]{2,0,1:T(8,128)(2,1)S(1)} all-to-all(bf16[32,16,416]{2,0,1:T(8,128)(2,1)S(1)} %copy.31), channel_id=1, replica_groups=mesh['seq'=16,'grp'=8] {'seq'}, dimensions={1} | all-to-all | bytes 851968 | tf_op jit(solution)/shard_map/all_to_all | solution.py:148
  162.6 2.3 convolution_convert_fusion
  164.9 3.8 %all-to-all-start.2 = ((bf16[16,32,1664]{2,1,0:T(8,128)(2,1)}), bf16[16,32,1664]{2,1,0:T(8,128)(2,1)S(1)}, u32[]{:S(2)}, u32[]{:S(2)}) async-start(bf16[16,32,1664]{2,1,0:T(8,128)(2,1)} %bitcast.178), calls=%async_computation.2 | async-start | bytes 3407872 | tf_op jit(solution)/shard_map/all_to_all | solution.py:150
  171.2 34.2 %all-to-all-done.2 = bf16[16,32,1664]{2,1,0:T(8,128)(2,1)S(1)} async-done(((bf16[16,32,1664]{2,1,0:T(8,128)(2,1)}), bf16[16,32,1664]{2,1,0:T(8,128)(2,1)S(1)}, u32[]{:S(2)}, u32[]{:S(2)}) %all-to-all-start.2) | async-done | bytes 1703968 | tf_op jit(solution)/shard_map/all_to_all | solution.py:150
  206.3 1.1 convolution_convert_fusion.3
  207.4 1.6 pad_maximum_fusion
  209.0 4.5 %all-to-all-start.3 = ((bf16[8,9,1664]{2,1,0:T(8,128)(2,1)}), bf16[8,9,1664]{2,1,0:T(8,128)(2,1)S(1)}, u32[]{:S(2)}, u32[]{:S(2)}) async-start(bf16[8,9,1664]{2,1,0:T(8,128)(2,1)} %pad_maximum_fusion), calls=%async_computation.3 | async-start | bytes 851968 | tf_op jit(solution)/shard_map/all_to_all | solution.py:172
  213.7 9.0 %all-to-all-done.3 = bf16[8,9,1664]{2,1,0:T(8,128)(2,1)S(1)} async-done(((bf16[8,9,1664]{2,1,0:T(8,128)(2,1)}), bf16[8,9,1664]{2,1,0:T(8,128)(2,1)S(1)}, u32[]{:S(2)}, u32[]{:S(2)}) %all-to-all-start.3) | async-done | bytes 239648 | tf_op jit(solution)/shard_map/all_to_all | solution.py:172
  225.1 58.3 %all-gather.11.cloned.1.call-done = bf16[2048,1664]{1,0:T(8,128)(2,1)} async-done(((bf16[128,1664]{1,0:T(8,128)(2,1)}), bf16[2048,1664]{1,0:T(8,128)(2,1)}) %all-gather.11.cloned.1.call-update) | async-done | bytes 6815760 | tf_op jit(solution)/shard_map/all_gather | solution.py:196
  283.3 5.7 %convolution_convert_fusion.1 = bf16[2048,312]{0,1:T(8,128)(2,1)S(1)} fusion(bf16[2048,1664]{1,0:T(8,128)(2,1)} %all-gather.11.cloned.1.call-done, bf16[1664,312]{0,1:T(8,128)(2,1)} %bitcast.190), kind=kOutput, calls=%fused_computation.37 | convolution fusion | flops 2127151104 | bytes 9132032 | tf_op jit(solution)/shard_map/dot_general | solution.py:29
  294.0 1.3 fusion.55
  297.0 15.5 %all_to_all.40 = bf16[16,128,104]{1,2,0:T(8,128)(2,1)S(1)} all-to-all(bf16[16,128,104]{1,2,0:T(8,128)(2,1)S(1)} %copy.36), channel_id=1, replica_groups=mesh['seq'=16,'grp'=8] {'seq'}, dimensions={0} | all-to-all | bytes 851968 | tf_op jit(solution)/shard_map/all_to_all | solution.py:66
  312.5 1.9 convolution_add_fusion
  (112 shorter events, 30.8 us)
Async XLA Ops:
  6.5 156.0 %copy-start = (bf16[416,1664]{1,0:T(8,128)(2,1)S(1)}, bf16[416,1664]{1,0:T(8,128)(2,1)}, u32[]{:S(2)}) copy-start(bf16[416,1664]{1,0:T(8,128)(2,1)} %param.21) | copy-start | bytes 4153348
  6.5 70.8 %all-gather.5.cloned.1.call-start = ((), (), s32[]{:S(2)}) async-start(), calls=%async_computation.5 | async-start | bytes 7241728 | tf_op jit(solution)/shard_map/all_gather | solution.py:125
  11.2 127.3 %all-gather.7.cloned.1.call-start = ((), (), s32[]{:S(2)}) async-start(), calls=%async_computation.6 | async-start | bytes 5883904 | tf_op jit(solution)/shard_map/all_gather | solution.py:123
  11.9 212.4 %all-gather.9.cloned.1.call-start = ((), (), s32[]{:S(2)}) async-start(), calls=%async_computation.7 | async-start | bytes 5883904 | tf_op jit(solution)/shard_map/all_gather | solution.py:138
  100.1 38.4 %copy-start.1 = (bf16[128,1664]{1,0:T(8,128)(2,1)S(1)}, bf16[128,1664]{1,0:T(8,128)(2,1)}, u32[]{:S(2)}) copy-start(bf16[128,1664]{1,0:T(8,128)(2,1)} %param.16) | copy-start | bytes 1277956
  101.3 37.2 %all-to-all-start = ((bf16[16,128,104]{1,2,0:T(8,128)(2,1)}), bf16[16,128,104]{1,2,0:T(8,128)(2,1)S(1)}, u32[]{:S(2)}, u32[]{:S(2)}) async-start(bf16[16,128,104]{1,2,0:T(8,128)(2,1)} %copy_bitcast_fusion), calls=%async_computation | async-start | bytes 851968 | tf_op jit(solution)/shard_map/all_to_all | solution.py:66
  138.5 4.0 %copy-start.3 = (f32[1664]{0:T(1024)S(1)}, f32[1664]{0:T(1024)}, u32[]{:S(2)}) copy-start(f32[1664]{0:T(1024)} %param.20) | copy-start | bytes 19972
  164.9 3.9 %copy-start.7 = (s32[32,1]{0,1:T(1,128)S(1)}, s32[32,1]{0,1:T(1,128)}, u32[]{:S(2)}) copy-start(s32[32,1]{0,1:T(1,128)} %param.23) | copy-start | bytes 388
  164.9 58.0 %copy-start.2 = (bf16[128,1664]{1,0:T(8,128)(2,1)S(1)}, bf16[128,1664]{1,0:T(8,128)(2,1)}, u32[]{:S(2)}) copy-start(bf16[128,1664]{1,0:T(8,128)(2,1)} %param.26) | copy-start | bytes 1277956
  164.9 40.5 %all-to-all-start.2 = ((bf16[16,32,1664]{2,1,0:T(8,128)(2,1)}), bf16[16,32,1664]{2,1,0:T(8,128)(2,1)S(1)}, u32[]{:S(2)}, u32[]{:S(2)}) async-start(bf16[16,32,1664]{2,1,0:T(8,128)(2,1)} %bitcast.178), calls=%async_computation.2 | async-start | bytes 3407872 | tf_op jit(solution)/shard_map/all_to_all | solution.py:150
  168.7 54.7 %copy-start.4 = (f32[1664]{0:T(1024)S(1)}, f32[1664]{0:T(1024)}, u32[]{:S(2)}) copy-start(f32[1664]{0:T(1024)} %param.27) | copy-start | bytes 19972
  168.9 44.8 %copy-start.8 = (s32[1,1,128]{2,1,0:T(1,128)S(1)}, s32[1,1,128]{2,1,0:T(1,128)}, u32[]{:S(2)}) copy-start(s32[1,1,128]{2,1,0:T(1,128)} %param.24) | copy-start | bytes 1540
  209.0 13.7 %all-to-all-start.3 = ((bf16[8,9,1664]{2,1,0:T(8,128)(2,1)}), bf16[8,9,1664]{2,1,0:T(8,128)(2,1)S(1)}, u32[]{:S(2)}, u32[]{:S(2)}) async-start(bf16[8,9,1664]{2,1,0:T(8,128)(2,1)} %pad_maximum_fusion), calls=%async_computation.3 | async-start | bytes 851968 | tf_op jit(solution)/shard_map/all_to_all | solution.py:172
  213.5 69.9 %all-gather.11.cloned.1.call-start = ((), (), s32[]{:S(2)}) async-start(), calls=%async_computation.8 | async-start | bytes 7241728 | tf_op jit(solution)/shard_map/all_gather | solution.py:196
  225.0 64.0 %copy-start.5 = (pred[2048]{0:T(1024)(128)(4,1)}, pred[2048]{0:T(1024)(128)(4,1)S(1)}, u32[]{:S(2)}) copy-start(pred[2048]{0:T(1024)(128)(4,1)S(1)} %iota_compare_fusion.4) | copy-start | bytes 6148
  289.4 0.7 slice-start.2
  291.2 0.7 copy-start.6
  295.4 17.2 %slice-start = ((s8[5537792]{0:T(1024)(128)(4,1)}), s8[1343488]{0:T(1024)(128)(4,1)S(1)}, s32[]{:S(2)}) async-start(s8[5537792]{0:T(1024)(128)(4,1)} %bitcast.175), calls=%async_computation.9 | async-start | bytes 2686976
  296.0 16.5 %slice-start.1 = ((s8[5537792]{0:T(1024)(128)(4,1)}), s8[4194304]{0:T(1024)(128)(4,1)S(1)}, s32[]{:S(2)}) async-start(s8[5537792]{0:T(1024)(128)(4,1)} %bitcast.175), calls=%async_computation.10 | async-start | bytes 8388608
Sparse Core Ops, SparseCore 0:
  11.3 66.0 all-gather.4
  79.5 58.9 all-gather.6
  140.6 70.9 all-gather.8
  224.5 58.8 all-gather.10
where the time goes:
time: 322 us; the launch traced here: 321 us
  waiting for transfers between devices  199 us (62%)
  matrix products  34.8 us (11%)
  blocking collectives  34.5 us (11%)
  other arithmetic  18.8 us (6%)
  between operations  14.1 us (4%)
  starting transfers between devices  13.8 us (4%)
  local copies, waits for them, and re-layouts  6.3 us (2%)
    all_gather x1, waiting for transfers between devices, per_device(): lax.all_gather(vis_normed, 'seq', axis=0, tiled=True)  64.4 us
    all_gather x1, waiting for transfers between devices, per_device(): lax.all_gather(txt_normed, 'seq', axis=0, tiled=True)  58.3 us
    all_to_all x1, waiting for transfers between devices, per_device(): lax.all_to_all(merge_partial.astype(jnp.bfloat16).reshape(seq_count, -1,...  34.2 us
    all_gather x1, waiting for transfers between devices, per_device(): vis_out_full = lax.all_gather(vis_out, 'seq', axis=0, tiled=True)  31.9 us
    all_to_all x1, blocking collectives, per_device(): lax.all_to_all(merged_in, 'seq', split_axis=1, concat_axis=0, tiled=True)  19 us
    all_to_all x1, blocking collectives, heads_to_rows(): lax.all_to_all(blocks, 'seq', split_axis=0, concat_axis=0, tiled=True)  15.5 us
    dot_general x2, matrix products, projector(): jnp.dot(shard_piece, packed, preferred_element_type=jnp.float32)  11.3 us
    all_to_all x1, waiting for transfers between devices, per_device(): lax.all_to_all(jnp.concatenate([outgoing, flag_row], axis=1), 'grp', spli...  9.02 us
  transfers between devices with their start and end apart: 7, of which 5 were waited for; matrix products, arithmetic and copies ran while one was open for 12% of the time, Pallas kernels for 0%

commit v1 on v0

--- a/solution.py
+++ b/solution.py
@@ -1,9 +1,36 @@
+import functools
 import jax
 import jax.numpy as jnp
 from jax import lax
 from jax.sharding import PartitionSpec as P
 
 HEAD_DIM = 104
+
+
+def part_block(vec, device_axis):
+    local_next = lax.axis_index(device_axis)
+    block_now = lax.axis_size(device_axis)
+    z_new, built, latest = (block_now, local_next, vec.shape[0])
+    vals = tuple((m * z_new if ix == 0 else m for ix, m in enumerate(vec.shape)))
+    arr_now = jnp.zeros(vals, vec.dtype)
+    formed = main = vec
+    block_out = lax.dynamic_update_slice_in_dim(arr_now, vec, built * latest, axis=0)
+    for idx in range(1, z_new // 2 + 1):
+        odd = tuple(((ix, (ix + 1) % z_new) for ix in range(z_new)))
+        formed = lax.ppermute(formed, device_axis, odd)
+        block_out = lax.dynamic_update_slice_in_dim(
+            block_out, formed, (built - idx) % z_new * latest, axis=0
+        )
+        if 2 * idx < z_new:
+            w1 = tuple(((ix, (ix - 1) % z_new) for ix in range(z_new)))
+            main = lax.ppermute(main, device_axis, w1)
+            block_out = lax.dynamic_update_slice_in_dim(
+                block_out, main, (built + idx) % z_new * latest, axis=0
+            )
+    return block_out
+
+
+push_groups = functools.partial(part_block, device_axis="seq")
 
 
 def layer_norm(row_block, scale_gain):
@@ -122,7 +149,7 @@
     group_patches = token_count * seq_count
     vis_out_full = lax.all_gather(vis_out, "seq", axis=0, tiled=True)
     vis_normed = layer_norm(patches, vis_gain).astype(jnp.bfloat16)
-    vis_proj = projector(vis_qkv, lax.all_gather(vis_normed, "seq", axis=0, tiled=True))
+    vis_proj = projector(vis_qkv, push_groups(vis_normed))
     bounds = jnp.cumsum(image_blocks[0])[:-1]
 
     def segment(indices):

time: 322 us -> 359 us (1.11)
  starting transfers between devices: 13.8 us -> 47.2 us
  waiting for transfers between devices: 199 us -> 183 us
  local copies, waits for them, and re-layouts: 6.3 us -> 21.2 us
  blocking collectives: 34.5 us -> 40.7 us
  other arithmetic: 18.8 us -> 14.6 us
    ppermute x0 -> x15, waiting for transfers between devices: none -> 77.1 us  [the longest x8 66.4 us: part_block(): formed = lax.ppermute(formed, device_axis, odd)]
    all_gather x1 -> x0, waiting for transfers between devices: 64.4 us -> none  [per_device(): lax.all_gather(vis_normed, 'seq', axis=0, tiled=True)]
    ppermute x0 -> x15, starting transfers between devices: none -> 38.8 us  [the longest x7 37.2 us: part_block(): main = lax.ppermute(main, device_axis, w1)]
    all_gather x1, waiting for transfers between devices: 31.9 us -> 0.01 us  [per_device(): vis_out_full = lax.all_gather(vis_out, 'seq', axis=0, tiled=True)]
    all_to_all x1 -> x2, blocking collectives: 15.5 us -> 27.6 us  [heads_to_rows(): lax.all_to_all(blocks, 'seq', split_axis=0, concat_axis=0, tiled=True)]
    dynamic_update_slice x0 -> x15, local copies, waits for them, and re-layouts: none -> 11.9 us  [the longest x8 6.37 us: part_block(): lax.dynamic_update_slice_in_dim(block_out, formed, (built - idx) % z_new...]
    all_to_all x1, blocking collectives: 19 us -> 13 us  [per_device(): lax.all_to_all(merged_in, 'seq', split_axis=1, concat_axis=0, tiled=True)]
    all_to_all x1 -> x0, starting transfers between devices: 5.26 us -> none  [heads_to_rows(): lax.all_to_all(blocks, 'seq', split_axis=0, concat_axis=0, tiled=True)]
  transfers between devices with their start and end apart: 7 -> 20, of which waited for: 5 -> 14; matrix products, arithmetic and copies ran while one was open for 12% -> 14% of each run, Pallas kernels for 0% -> 0%
where the time goes in v1:
time: 359 us; the launch traced here: 358 us
  waiting for transfers between devices  183 us (51%)
  starting transfers between devices  47.2 us (13%)
  blocking collectives  40.7 us (11%)
  matrix products  37.3 us (10%)
  local copies, waits for them, and re-layouts  21.2 us (6%)
  other arithmetic  14.6 us (4%)
  between operations  14.4 us (4%)
    ppermute x8, waiting for transfers between devices, part_block(): formed = lax.ppermute(formed, device_axis, odd)  66.4 us
    all_gather x1, waiting for transfers between devices, per_device(): lax.all_gather(txt_normed, 'seq', axis=0, tiled=True)  58.5 us
    all_to_all x1, waiting for transfers between devices, per_device(): lax.all_to_all(merge_partial.astype(jnp.bfloat16).reshape(seq_count, -1,...  38.2 us
    ppermute x7, starting transfers between devices, part_block(): main = lax.ppermute(main, device_axis, w1)  37.2 us
    all_to_all x2, blocking collectives, heads_to_rows(): lax.all_to_all(blocks, 'seq', split_axis=0, concat_axis=0, tiled=True)  27.6 us
    all_to_all x1, blocking collectives, per_device(): lax.all_to_all(merged_in, 'seq', split_axis=1, concat_axis=0, tiled=True)  13 us
    dot_general x2, matrix products, projector(): jnp.dot(shard_piece, packed, preferred_element_type=jnp.float32)  11.1 us
    ppermute x7, waiting for transfers between devices, part_block(): main = lax.ppermute(main, device_axis, w1)  10.6 us
  transfers between devices with their start and end apart: 20, of which 14 were waited for; matrix products, arithmetic and copies ran while one was open for 14% of the time, Pallas kernels for 0%

profile of v1, /device:TPU:0, one launch (start us, length us, event | category | flops | bytes accessed | tf_op | source)
XLA Modules:
  0.0 358.0 jit_solution(9299421530355107676)
XLA Ops:
  19.4 9.2 %collective-permute-done = bf16[128,1664]{1,0:T(8,128)(2,1)S(1)} collective-permute-done((bf16[128,1664]{1,0:T(8,128)(2,1)S(1)}, bf16[128,1664]{1,0:T(8,128)(2,1)S(1)}, u32[]{:S(2)}, u32[]{:S(2)}) %collective-permute-start) | collective-permute-done | bytes 426016 | tf_op jit(solution)/shard_map/ppermute | solution.py:20
  28.6 5.3 %collective-permute-start.3 = (bf16[128,1664]{1,0:T(8,128)(2,1)S(1)}, bf16[128,1664]{1,0:T(8,128)(2,1)S(1)}, u32[]{:S(2)}, u32[]{:S(2)}) collective-permute-start(bf16[128,1664]{1,0:T(8,128)(2,1)S(1)} %collective-permute-done.1), channel_id=1, source_target_pairs={{0,120},{8,0},{16,8},{24,16},{32,24},{40,32},{48,40},{56,48},{64,5... | collective-permute-start | bytes 1277960 | tf_op jit(solution)/shard_map/ppermute | solution.py:26
  35.5 12.9 %collective-permute-done.2 = bf16[128,1664]{1,0:T(8,128)(2,1)S(1)} collective-permute-done((bf16[128,1664]{1,0:T(8,128)(2,1)S(1)}, bf16[128,1664]{1,0:T(8,128)(2,1)S(1)}, u32[]{:S(2)}, u32[]{:S(2)}) %collective-permute-start.2) | collective-permute-done | bytes 426016 | tf_op jit(solution)/shard_map/ppermute | solution.py:20
  48.5 5.3 %collective-permute-start.5 = (bf16[128,1664]{1,0:T(8,128)(2,1)S(1)}, bf16[128,1664]{1,0:T(8,128)(2,1)S(1)}, u32[]{:S(2)}, u32[]{:S(2)}) collective-permute-start(bf16[128,1664]{1,0:T(8,128)(2,1)S(1)} %collective-permute-done.3), channel_id=1, source_target_pairs={{0,120},{8,0},{16,8},{24,16},{32,24},{40,32},{48,40},{56,48},{64,5... | collective-permute-start | bytes 1277960 | tf_op jit(solution)/shard_map/ppermute | solution.py:26
  55.4 9.2 %collective-permute-done.4 = bf16[128,1664]{1,0:T(8,128)(2,1)S(1)} collective-permute-done((bf16[128,1664]{1,0:T(8,128)(2,1)S(1)}, bf16[128,1664]{1,0:T(8,128)(2,1)S(1)}, u32[]{:S(2)}, u32[]{:S(2)}) %collective-permute-start.4) | collective-permute-done | bytes 426016 | tf_op jit(solution)/shard_map/ppermute | solution.py:20
  64.6 5.1 %collective-permute-done.5 = bf16[128,1664]{1,0:T(8,128)(2,1)S(1)} collective-permute-done((bf16[128,1664]{1,0:T(8,128)(2,1)S(1)}, bf16[128,1664]{1,0:T(8,128)(2,1)S(1)}, u32[]{:S(2)}, u32[]{:S(2)}) %collective-permute-start.5) | collective-permute-done | bytes 426016 | tf_op jit(solution)/shard_map/ppermute | solution.py:26
  69.7 5.8 %collective-permute-start.7 = (bf16[128,1664]{1,0:T(8,128)(2,1)S(1)}, bf16[128,1664]{1,0:T(8,128)(2,1)S(1)}, u32[]{:S(2)}, u32[]{:S(2)}) collective-permute-start(bf16[128,1664]{1,0:T(8,128)(2,1)S(1)} %collective-permute-done.5), channel_id=1, source_target_pairs={{0,120},{8,0},{16,8},{24,16},{32,24},{40,32},{48,40},{56,48},{64,5... | collective-permute-start | bytes 1277960 | tf_op jit(solution)/shard_map/ppermute | solution.py:26
  77.1 11.2 %collective-permute-done.6 = bf16[128,1664]{1,0:T(8,128)(2,1)S(1)} collective-permute-done((bf16[128,1664]{1,0:T(8,128)(2,1)S(1)}, bf16[128,1664]{1,0:T(8,128)(2,1)S(1)}, u32[]{:S(2)}, u32[]{:S(2)}) %collective-permute-start.6) | collective-permute-done | bytes 426016 | tf_op jit(solution)/shard_map/ppermute | solution.py:20
  88.3 4.5 %collective-permute-done.7 = bf16[128,1664]{1,0:T(8,128)(2,1)S(1)} collective-permute-done((bf16[128,1664]{1,0:T(8,128)(2,1)S(1)}, bf16[128,1664]{1,0:T(8,128)(2,1)S(1)}, u32[]{:S(2)}, u32[]{:S(2)}) %collective-permute-start.7) | collective-permute-done | bytes 426016 | tf_op jit(solution)/shard_map/ppermute | solution.py:26
  92.8 5.8 %collective-permute-start.9 = (bf16[128,1664]{1,0:T(8,128)(2,1)S(1)}, bf16[128,1664]{1,0:T(8,128)(2,1)S(1)}, u32[]{:S(2)}, u32[]{:S(2)}) collective-permute-start(bf16[128,1664]{1,0:T(8,128)(2,1)S(1)} %collective-permute-done.7), channel_id=1, source_target_pairs={{0,120},{8,0},{16,8},{24,16},{32,24},{40,32},{48,40},{56,48},{64,5... | collective-permute-start | bytes 1277960 | tf_op jit(solution)/shard_map/ppermute | solution.py:26
  104.3 5.8 %collective-permute-start.11 = (bf16[128,1664]{1,0:T(8,128)(2,1)S(1)}, bf16[128,1664]{1,0:T(8,128)(2,1)S(1)}, u32[]{:S(2)}, u32[]{:S(2)}) collective-permute-start(bf16[128,1664]{1,0:T(8,128)(2,1)S(1)} %collective-permute-done.9), channel_id=1, source_target_pairs={{0,120},{8,0},{16,8},{24,16},{32,24},{40,32},{48,40},{56,48},{64,5... | collective-permute-start | bytes 1277960 | tf_op jit(solution)/shard_map/ppermute | solution.py:26
  111.7 5.1 %collective-permute-done.10 = bf16[128,1664]{1,0:T(8,128)(2,1)S(1)} collective-permute-done((bf16[128,1664]{1,0:T(8,128)(2,1)S(1)}, bf16[128,1664]{1,0:T(8,128)(2,1)S(1)}, u32[]{:S(2)}, u32[]{:S(2)}) %collective-permute-start.10) | collective-permute-done | bytes 426016 | tf_op jit(solution)/shard_map/ppermute | solution.py:20
  116.7 5.3 %collective-permute-start.13 = (bf16[128,1664]{1,0:T(8,128)(2,1)S(1)}, bf16[128,1664]{1,0:T(8,128)(2,1)S(1)}, u32[]{:S(2)}, u32[]{:S(2)}) collective-permute-start(bf16[128,1664]{1,0:T(8,128)(2,1)S(1)} %collective-permute-done.11), channel_id=1, source_target_pairs={{0,120},{8,0},{16,8},{24,16},{32,24},{40,32},{48,40},{56,48},{64,5... | collective-permute-start | bytes 1277960 | tf_op jit(solution)/shard_map/ppermute | solution.py:26
  123.6 5.7 %collective-permute-done.12 = bf16[128,1664]{1,0:T(8,128)(2,1)S(1)} collective-permute-done((bf16[128,1664]{1,0:T(8,128)(2,1)S(1)}, bf16[128,1664]{1,0:T(8,128)(2,1)S(1)}, u32[]{:S(2)}, u32[]{:S(2)}) %collective-permute-start.12) | collective-permute-done | bytes 426016 | tf_op jit(solution)/shard_map/ppermute | solution.py:20
  131.0 10.2 %collective-permute-done.14 = bf16[128,1664]{1,0:T(8,128)(2,1)S(1)} collective-permute-done((bf16[128,1664]{1,0:T(8,128)(2,1)S(1)}, bf16[128,1664]{1,0:T(8,128)(2,1)S(1)}, u32[]{:S(2)}, u32[]{:S(2)}) %collective-permute-start.14) | collective-permute-done | bytes 426016 | tf_op jit(solution)/shard_map/ppermute | solution.py:20
  141.9 5.5 %convolution_convert_fusion.2 = bf16[2048,312]{0,1:T(8,128)(2,1)S(1)} fusion(bf16[2048,1664]{1,0:T(8,128)(2,1)} %constant_dynamic-update-slice_fusion, bf16[1664,312]{0,1:T(8,128)(2,1)S(1)} %bitcast.189), kind=kOutput, calls=%fused_computation.38 | convolution fusion | flops 2127151104 | bytes 9132032 | tf_op jit(solution)/shard_map/dot_general | solution.py:56
  147.9 19.5 %while.12 = (s32[]{:T(128)}, bf16[4,512,1,104]{1,3,2,0:T(8,128)(2,1)}, s32[4]{0:T(128)S(1)}, s32[3]{0:T(128)S(1)}, s32[2048]{0:T(1024)S(1)}, /*index=5*/bf16[4,5...) while((s32[]{:T(128)}, ...), condition=%wide.region_10.11_spmd, body=%wide.region_6.10_spmd.sunk | while | flops 445709312 | bytes 13675133 | solution.py:85
  168.7 12.2 %all_to_all.39 = bf16[16,128,104]{1,2,0:T(8,128)(2,1)S(1)} all-to-all(bf16[16,128,104]{1,2,0:T(8,128)(2,1)S(1)} %copy_bitcast_fusion), channel_id=1, replica_groups=mesh['seq'=16,'grp'=8] {'seq'}, dimensions={0} | all-to-all | bytes 851968 | tf_op jit(solution)/shard_map/all_to_all | solution.py:93
  186.1 13.0 %all_to_all.40 = bf16[32,16,416]{2,0,1:T(8,128)(2,1)S(1)} all-to-all(bf16[32,16,416]{2,0,1:T(8,128)(2,1)S(1)} %copy.31), channel_id=1, replica_groups=mesh['seq'=16,'grp'=8] {'seq'}, dimensions={1} | all-to-all | bytes 851968 | tf_op jit(solution)/shard_map/all_to_all | solution.py:175
  205.8 38.2 %all-to-all-done.2 = bf16[16,32,1664]{2,1,0:T(8,128)(2,1)S(1)} async-done(((bf16[16,32,1664]{2,1,0:T(8,128)(2,1)}), bf16[16,32,1664]{2,1,0:T(8,128)(2,1)S(1)}, u32[]{:S(2)}, u32[]{:S(2)}) %all-to-all-start.2) | async-done | bytes 1703968 | tf_op jit(solution)/shard_map/all_to_all | solution.py:177
  249.7 9.0 %all-to-all-done.3 = bf16[8,9,1664]{2,1,0:T(8,128)(2,1)S(1)} async-done(((bf16[8,9,1664]{2,1,0:T(8,128)(2,1)}), bf16[8,9,1664]{2,1,0:T(8,128)(2,1)S(1)}, u32[]{:S(2)}, u32[]{:S(2)}) %all-to-all-start.3) | async-done | bytes 239648 | tf_op jit(solution)/shard_map/all_to_all | solution.py:199
  262.1 58.5 %all-gather.8.cloned.1.call-done = bf16[2048,1664]{1,0:T(8,128)(2,1)} async-done(((bf16[128,1664]{1,0:T(8,128)(2,1)}), bf16[2048,1664]{1,0:T(8,128)(2,1)}) %all-gather.8.cloned.1.call-update) | async-done | bytes 6815760 | tf_op jit(solution)/shard_map/all_gather | solution.py:223
  320.6 5.7 %convolution_convert_fusion.1 = bf16[2048,312]{0,1:T(8,128)(2,1)S(1)} fusion(bf16[2048,1664]{1,0:T(8,128)(2,1)} %all-gather.8.cloned.1.call-done, bf16[1664,312]{0,1:T(8,128)(2,1)} %bitcast.190), kind=kOutput, calls=%fused_computation.37 | convolution fusion | flops 2127151104 | bytes 9132032 | tf_op jit(solution)/shard_map/dot_general | solution.py:56
  334.1 15.5 %all_to_all.41 = bf16[16,128,104]{1,2,0:T(8,128)(2,1)S(1)} all-to-all(bf16[16,128,104]{1,2,0:T(8,128)(2,1)S(1)} %copy.36), channel_id=1, replica_groups=mesh['seq'=16,'grp'=8] {'seq'}, dimensions={0} | all-to-all | bytes 851968 | tf_op jit(solution)/shard_map/all_to_all | solution.py:93
  (158 shorter events, 79.8 us)
Async XLA Ops:
  6.5 192.6 %copy-start = (bf16[416,1664]{1,0:T(8,128)(2,1)S(1)}, bf16[416,1664]{1,0:T(8,128)(2,1)}, u32[]{:S(2)}) copy-start(bf16[416,1664]{1,0:T(8,128)(2,1)} %param.21) | copy-start | bytes 4153348
  6.5 174.4 %all-gather.4.cloned.1.call-start = ((), (), s32[]{:S(2)}) async-start(), calls=%async_computation.5 | async-start | bytes 5883904 | tf_op jit(solution)/shard_map/all_gather | solution.py:150
  13.5 15.1 %collective-permute-start = (bf16[128,1664]{1,0:T(8,128)(2,1)S(1)}, bf16[128,1664]{1,0:T(8,128)(2,1)S(1)}, u32[]{:S(2)}, u32[]{:S(2)}) collective-permute-start(bf16[128,1664]{1,0:T(8,128)(2,1)S(1)} %get-tuple-element.149), channel_id=1, source_target_pairs={{0,8},{8,16},{16,24},{24,32},{32,40},{40,48},{48,56},{56,64},{64,7... | collective-permute-start | bytes 1277960 | tf_op jit(solution)/shard_map/ppermute | solution.py:20
  15.1 13.5 %collective-permute-start.1 = (bf16[128,1664]{1,0:T(8,128)(2,1)S(1)}, bf16[128,1664]{1,0:T(8,128)(2,1)S(1)}, u32[]{:S(2)}, u32[]{:S(2)}) collective-permute-start(bf16[128,1664]{1,0:T(8,128)(2,1)S(1)} %get-tuple-element.149), channel_id=1, source_target_pairs={{0,120},{8,0},{16,8},{24,16},{32,24},{40,32},{48,40},{56,48},{64,5... | collective-permute-start | bytes 1277960 | tf_op jit(solution)/shard_map/ppermute | solution.py:26
  18.8 242.5 %all-gather.6.cloned.1.call-start = ((), (), s32[]{:S(2)}) async-start(), calls=%async_computation.6 | async-start | bytes 5883904 | tf_op jit(solution)/shard_map/all_gather | solution.py:165
  28.6 19.8 %collective-permute-start.2 = (bf16[128,1664]{1,0:T(8,128)(2,1)S(1)}, bf16[128,1664]{1,0:T(8,128)(2,1)S(1)}, u32[]{:S(2)}, u32[]{:S(2)}) collective-permute-start(bf16[128,1664]{1,0:T(8,128)(2,1)S(1)} %collective-permute-done), channel_id=1, source_target_pairs={{0,8},{8,16},{16,24},{24,32},{32,40},{40,48},{48,56},{56,64},{64,7... | collective-permute-start | bytes 1277960 | tf_op jit(solution)/shard_map/ppermute | solution.py:20
  28.6 19.8 %collective-permute-start.3 = (bf16[128,1664]{1,0:T(8,128)(2,1)S(1)}, bf16[128,1664]{1,0:T(8,128)(2,1)S(1)}, u32[]{:S(2)}, u32[]{:S(2)}) collective-permute-start(bf16[128,1664]{1,0:T(8,128)(2,1)S(1)} %collective-permute-done.1), channel_id=1, source_target_pairs={{0,120},{8,0},{16,8},{24,16},{32,24},{40,32},{48,40},{56,48},{64,5... | collective-permute-start | bytes 1277960 | tf_op jit(solution)/shard_map/ppermute | solution.py:26
  48.4 16.2 %collective-permute-start.4 = (bf16[128,1664]{1,0:T(8,128)(2,1)S(1)}, bf16[128,1664]{1,0:T(8,128)(2,1)S(1)}, u32[]{:S(2)}, u32[]{:S(2)}) collective-permute-start(bf16[128,1664]{1,0:T(8,128)(2,1)S(1)} %collective-permute-done.2), channel_id=1, source_target_pairs={{0,8},{8,16},{16,24},{24,32},{32,40},{40,48},{48,56},{56,64},{64,7... | collective-permute-start | bytes 1277960 | tf_op jit(solution)/shard_map/ppermute | solution.py:20
  48.5 21.2 %collective-permute-start.5 = (bf16[128,1664]{1,0:T(8,128)(2,1)S(1)}, bf16[128,1664]{1,0:T(8,128)(2,1)S(1)}, u32[]{:S(2)}, u32[]{:S(2)}) collective-permute-start(bf16[128,1664]{1,0:T(8,128)(2,1)S(1)} %collective-permute-done.3), channel_id=1, source_target_pairs={{0,120},{8,0},{16,8},{24,16},{32,24},{40,32},{48,40},{56,48},{64,5... | collective-permute-start | bytes 1277960 | tf_op jit(solution)/shard_map/ppermute | solution.py:26
  64.6 23.7 %collective-permute-start.6 = (bf16[128,1664]{1,0:T(8,128)(2,1)S(1)}, bf16[128,1664]{1,0:T(8,128)(2,1)S(1)}, u32[]{:S(2)}, u32[]{:S(2)}) collective-permute-start(bf16[128,1664]{1,0:T(8,128)(2,1)S(1)} %collective-permute-done.4), channel_id=1, source_target_pairs={{0,8},{8,16},{16,24},{24,32},{32,40},{40,48},{48,56},{56,64},{64,7... | collective-permute-start | bytes 1277960 | tf_op jit(solution)/shard_map/ppermute | solution.py:20
  69.7 23.1 %collective-permute-start.7 = (bf16[128,1664]{1,0:T(8,128)(2,1)S(1)}, bf16[128,1664]{1,0:T(8,128)(2,1)S(1)}, u32[]{:S(2)}, u32[]{:S(2)}) collective-permute-start(bf16[128,1664]{1,0:T(8,128)(2,1)S(1)} %collective-permute-done.5), channel_id=1, source_target_pairs={{0,120},{8,0},{16,8},{24,16},{32,24},{40,32},{48,40},{56,48},{64,5... | collective-permute-start | bytes 1277960 | tf_op jit(solution)/shard_map/ppermute | solution.py:26
  76.3 65.6 %copy-start.8 = (bf16[3,1664,104]{1,2,0:T(8,128)(2,1)S(1)}, bf16[3,1664,104]{1,2,0:T(8,128)(2,1)}, u32[]{:S(2)}) copy-start(bf16[3,1664,104]{1,2,0:T(8,128)(2,1)} %param.18) | copy-start | bytes 3115012
  88.3 14.9 %collective-permute-start.8 = (bf16[128,1664]{1,0:T(8,128)(2,1)S(1)}, bf16[128,1664]{1,0:T(8,128)(2,1)S(1)}, u32[]{:S(2)}, u32[]{:S(2)}) collective-permute-start(bf16[128,1664]{1,0:T(8,128)(2,1)S(1)} %collective-permute-done.6), channel_id=1, source_target_pairs={{0,8},{8,16},{16,24},{24,32},{32,40},{40,48},{48,56},{56,64},{64,7... | collective-permute-start | bytes 1277960 | tf_op jit(solution)/shard_map/ppermute | solution.py:20
  92.8 11.4 %collective-permute-start.9 = (bf16[128,1664]{1,0:T(8,128)(2,1)S(1)}, bf16[128,1664]{1,0:T(8,128)(2,1)S(1)}, u32[]{:S(2)}, u32[]{:S(2)}) collective-permute-start(bf16[128,1664]{1,0:T(8,128)(2,1)S(1)} %collective-permute-done.7), channel_id=1, source_target_pairs={{0,120},{8,0},{16,8},{24,16},{32,24},{40,32},{48,40},{56,48},{64,5... | collective-permute-start | bytes 1277960 | tf_op jit(solution)/shard_map/ppermute | solution.py:26
  103.2 13.5 %collective-permute-start.10 = (bf16[128,1664]{1,0:T(8,128)(2,1)S(1)}, bf16[128,1664]{1,0:T(8,128)(2,1)S(1)}, u32[]{:S(2)}, u32[]{:S(2)}) collective-permute-start(bf16[128,1664]{1,0:T(8,128)(2,1)S(1)} %collective-permute-done.8), channel_id=1, source_target_pairs={{0,8},{8,16},{16,24},{24,32},{32,40},{40,48},{48,56},{56,64},{64,7... | collective-permute-start | bytes 1277960 | tf_op jit(solution)/shard_map/ppermute | solution.py:20
  104.3 12.5 %collective-permute-start.11 = (bf16[128,1664]{1,0:T(8,128)(2,1)S(1)}, bf16[128,1664]{1,0:T(8,128)(2,1)S(1)}, u32[]{:S(2)}, u32[]{:S(2)}) collective-permute-start(bf16[128,1664]{1,0:T(8,128)(2,1)S(1)} %collective-permute-done.9), channel_id=1, source_target_pairs={{0,120},{8,0},{16,8},{24,16},{32,24},{40,32},{48,40},{56,48},{64,5... | collective-permute-start | bytes 1277960 | tf_op jit(solution)/shard_map/ppermute | solution.py:26
  116.7 12.6 %collective-permute-start.12 = (bf16[128,1664]{1,0:T(8,128)(2,1)S(1)}, bf16[128,1664]{1,0:T(8,128)(2,1)S(1)}, u32[]{:S(2)}, u32[]{:S(2)}) collective-permute-start(bf16[128,1664]{1,0:T(8,128)(2,1)S(1)} %collective-permute-done.10), channel_id=1, source_target_pairs={{0,8},{8,16},{16,24},{24,32},{32,40},{40,48},{48,56},{56,64},{64,7... | collective-permute-start | bytes 1277960 | tf_op jit(solution)/shard_map/ppermute | solution.py:20
  116.7 13.4 %collective-permute-start.13 = (bf16[128,1664]{1,0:T(8,128)(2,1)S(1)}, bf16[128,1664]{1,0:T(8,128)(2,1)S(1)}, u32[]{:S(2)}, u32[]{:S(2)}) collective-permute-start(bf16[128,1664]{1,0:T(8,128)(2,1)S(1)} %collective-permute-done.11), channel_id=1, source_target_pairs={{0,120},{8,0},{16,8},{24,16},{32,24},{40,32},{48,40},{56,48},{64,5... | collective-permute-start | bytes 1277960 | tf_op jit(solution)/shard_map/ppermute | solution.py:26
  129.3 11.8 %collective-permute-start.14 = (bf16[128,1664]{1,0:T(8,128)(2,1)S(1)}, bf16[128,1664]{1,0:T(8,128)(2,1)S(1)}, u32[]{:S(2)}, u32[]{:S(2)}) collective-permute-start(bf16[128,1664]{1,0:T(8,128)(2,1)S(1)} %collective-permute-done.12), channel_id=1, source_target_pairs={{0,8},{8,16},{16,24},{24,32},{32,40},{40,48},{48,56},{56,64},{64,7... | collective-permute-start | bytes 1277960 | tf_op jit(solution)/shard_map/ppermute | solution.py:20
  201.4 59.0 %copy-start.4 = (f32[1664]{0:T(1024)S(1)}, f32[1664]{0:T(1024)}, u32[]{:S(2)}) copy-start(f32[1664]{0:T(1024)} %param.27) | copy-start | bytes 19972
  201.4 42.5 %all-to-all-start.2 = ((bf16[16,32,1664]{2,1,0:T(8,128)(2,1)}), bf16[16,32,1664]{2,1,0:T(8,128)(2,1)S(1)}, u32[]{:S(2)}, u32[]{:S(2)}) async-start(bf16[16,32,1664]{2,1,0:T(8,128)(2,1)} %bitcast.178), calls=%async_computation.2 | async-start | bytes 3407872 | tf_op jit(solution)/shard_map/all_to_all | solution.py:177
  245.2 13.5 %all-to-all-start.3 = ((bf16[8,9,1664]{2,1,0:T(8,128)(2,1)}), bf16[8,9,1664]{2,1,0:T(8,128)(2,1)S(1)}, u32[]{:S(2)}, u32[]{:S(2)}) async-start(bf16[8,9,1664]{2,1,0:T(8,128)(2,1)} %pad_maximum_fusion), calls=%async_computation.3 | async-start | bytes 851968 | tf_op jit(solution)/shard_map/all_to_all | solution.py:199
  249.5 71.1 %all-gather.8.cloned.1.call-start = ((), (), s32[]{:S(2)}) async-start(), calls=%async_computation.7 | async-start | bytes 7241728 | tf_op jit(solution)/shard_map/all_gather | solution.py:223
  262.0 64.2 %copy-start.5 = (pred[2048]{0:T(1024)(128)(4,1)}, pred[2048]{0:T(1024)(128)(4,1)S(1)}, u32[]{:S(2)}) copy-start(pred[2048]{0:T(1024)(128)(4,1)S(1)} %iota_compare_fusion.4) | copy-start | bytes 6148
  (10 other events, 115.5 us)
Sparse Core Ops, SparseCore 0:
  19.0 79.1 all-gather.3
  168.8 73.1 all-gather.5
  261.5 59.0 all-gather.7
